TPU v7x, 128 devices: a whole 4x4x4 slice. The times are simulated.
128 devices in a mesh: tm: 4 (over y_hi, core), space: 32 (over x, y_lo, z).
Axes of the slice: x: 4, y: 4 (y_hi: 2, y_lo: 2; y = y_hi * 2 + y_lo), z: 4, core: 2. Of those that a mesh axis runs over, the one named last changes fastest.
Arguments:
- query_rows: bfloat16 [32768, 2560], P(('tm', 'space')), may hold values from -18 to 18
- key_rows: bfloat16 [32768, 2560], P(('tm', 'space')), may hold values from -7 to 7
- value_rows: bfloat16 [32768, 2560], P(('tm', 'space')), may hold values from -12 to 12
- out_cotangent: bfloat16 [32768, 2560], P(('tm', 'space')), may hold values from -12 to 12
- tile_slot: int32 [32768], P(('tm', 'space')), may hold values from 0 to 32767, as said below
- window_reach: int32 [4, 32, 2], P(None, 'space'), may hold values from 0 to 1, as said below
Outputs:
- attended: bfloat16 [32768, 2560], P(('tm', 'space'))
- query_grad: bfloat16 [32768, 2560], P(('tm', 'space'))
- key_grad: bfloat16 [32768, 2560], P(('tm', 'space'))
- value_grad: bfloat16 [32768, 2560], P(('tm', 'space'))
Inputs may be any that keep to these rules, and one draw needn't show every extreme that they name: `tile_slot`: A permutation of the tile-order positions. The raster tokens r * 256 to r * 256 + 256 - 1 (shard r, counted over tm first, then space) take, for every shard d, exactly the 2 positions d * 256 + r * 2 to d * 256 + r * 2 + 1. `window_reach`: entry 0 is 0 in the lowest slab and entry 1 is 0 in the highest slab.
All inputs are finite; a program needn't handle non-finite values.
Results may differ from a plain program's by a relative error of at most 0.0053.
Values may be sent and summed in bfloat16 or wider, within the bound.
No kernel may reach another device: no remote copies, remote signals or barrier semaphores. Data moves between devices by JAX's collectives and lax.ppermute only.
A program may use at most 192 MiB of HBM per device.

v0:
```python
import jax
import jax.numpy as jnp
from jax import lax
from jax.sharding import PartitionSpec as P

H = 20
HD = 128
TILE = 256


def extended_2(cells, sides, width):
    for axis, dim in sides:
        count = lax.axis_size(axis)
        ends = count - 1
        head = lax.slice_in_dim(cells, 0, width, axis=dim)
        tail = lax.slice_in_dim(cells, cells.shape[dim] - width, cells.shape[dim], axis=dim)
        cells = jnp.concatenate(
            [
                lax.ppermute(tail, axis, [(i, (i + 1) % count) for i in range(ends)]),
                cells,
                lax.ppermute(head, axis, [((i + 1) % count, i) for i in range(ends)]),
            ],
            axis=dim,
        )
    return cells


def passed_along(block, axis, distance):
    devices = range(lax.axis_size(axis))
    route = [(i - distance, i) for i in devices if i - distance in devices]
    return lax.ppermute(block, axis, route)


def slice_channels(array, column, block_width):
    return lax.dynamic_slice_in_dim(array, column, block_width, array.ndim - 1)


def head_blocking():
    heads_block = max((divisor for divisor in range(1, 6) if H % divisor == 0))
    return (heads_block, heads_block * HD, H // heads_block)


def five_sets(extended):
    picks = [
        extended[:, 0, 1:-1],
        extended[:, 1, 1:-1],
        extended[:, 2, 1:-1],
        extended[:, 1, :-2],
        extended[:, 1, 2:],
    ]
    return jnp.stack(picks, axis=1)


def attend_all(query_tile, grad_tile, near_keys, near_values, allowed, keep_range):
    tokens_here, channels = query_tile.shape
    tiles_here = tokens_here // TILE
    sets_count = near_keys.shape[0]
    heads_block, block_width, block_count = head_blocking()
    softmax_scale = HD ** (-0.5)
    visible = allowed[:, None, None, :, None]
    keep_low, keep_high = keep_range
    terms_count = keep_high - keep_low
    shape_query = (tiles_here, TILE, heads_block, HD)
    shape_keys = (sets_count, tiles_here, TILE, heads_block, HD)
    initial = (
        jnp.zeros((tokens_here, channels), jnp.bfloat16),
        jnp.zeros((tokens_here, channels), jnp.bfloat16),
        jnp.zeros((terms_count, tokens_here, channels), jnp.float32),
        jnp.zeros((terms_count, tokens_here, channels), jnp.float32),
        jnp.zeros((3, tiles_here, H, TILE), jnp.float32),
    )

    def attend_block_step(step_index, carry):
        attended, query_grad, key_terms, value_terms, row_stats = carry
        column = step_index * block_width
        head_start = step_index * heads_block
        queries = slice_channels(query_tile, column, block_width).reshape(shape_query)
        cotangent = slice_channels(grad_tile, column, block_width).reshape(shape_query)
        keys_block = slice_channels(near_keys, column, block_width).reshape(shape_keys)
        values_block = slice_channels(near_values, column, block_width).reshape(shape_keys)
        scores = (
            jnp.einsum("tqhd,atkhd->thqak", queries, keys_block, preferred_element_type=jnp.float32)
            * softmax_scale
        )
        row_max = jnp.max(jnp.where(visible, scores, -1e30), axis=(3, 4), keepdims=True)
        expo = jnp.where(visible, jnp.exp(scores - row_max), 0.0)
        row_sum = jnp.sum(expo, axis=(3, 4), keepdims=True)
        weights = expo / row_sum
        weights_low = weights.astype(jnp.bfloat16)
        output = jnp.einsum(
            "thqak,atkhd->tqhd", weights_low, values_block, preferred_element_type=jnp.float32
        )
        dweights = jnp.einsum(
            "tqhd,atkhd->thqak", cotangent, values_block, preferred_element_type=jnp.float32
        )
        row_dot = jnp.sum(weights * dweights, axis=(3, 4), keepdims=True)
        dscores = (weights * (dweights - row_dot) * softmax_scale).astype(jnp.bfloat16)
        query_part = jnp.einsum(
            "thqak,atkhd->tqhd", dscores, keys_block, preferred_element_type=jnp.float32
        )
        key_part = jnp.einsum(
            "thqak,tqhd->atkhd",
            dscores[:, :, :, keep_low:keep_high],
            queries,
            preferred_element_type=jnp.float32,
        )
        value_part = jnp.einsum(
            "thqak,tqhd->atkhd",
            weights_low[:, :, :, keep_low:keep_high],
            cotangent,
            preferred_element_type=jnp.float32,
        )
        attended = lax.dynamic_update_slice_in_dim(
            attended, output.reshape(tokens_here, block_width).astype(jnp.bfloat16), column, 1
        )
        query_grad = lax.dynamic_update_slice_in_dim(
            query_grad, query_part.reshape(tokens_here, block_width).astype(jnp.bfloat16), column, 1
        )
        key_terms = lax.dynamic_update_slice_in_dim(
            key_terms, key_part.reshape(terms_count, tokens_here, block_width), column, 2
        )
        value_terms = lax.dynamic_update_slice_in_dim(
            value_terms, value_part.reshape(terms_count, tokens_here, block_width), column, 2
        )
        block_stats = jnp.stack([row_max, row_sum, row_dot]).reshape(
            3, tiles_here, heads_block, TILE
        )
        row_stats = lax.dynamic_update_slice_in_dim(row_stats, block_stats, head_start, 2)
        return (attended, query_grad, key_terms, value_terms, row_stats)

    return lax.fori_loop(0, block_count, attend_block_step, initial)


def neighbour_terms(near_rows, near_stats, key_tile, value_tile, includes, key_start, value_start):
    tokens_here, channels = key_tile.shape
    tiles_here = tokens_here // TILE
    heads_block, block_width, block_count = head_blocking()
    softmax_scale = HD ** (-0.5)
    shape_rows = (tiles_here, TILE, heads_block, HD)

    def neighbour_block_step(step_index, carry):
        key_total, value_total = carry
        column = step_index * block_width
        head_start = step_index * heads_block
        keys_block = slice_channels(key_tile, column, block_width).reshape(shape_rows)
        values_block = slice_channels(value_tile, column, block_width).reshape(shape_rows)
        key_sum = jnp.zeros(shape_rows, jnp.float32)
        value_sum = jnp.zeros(shape_rows, jnp.float32)
        for near_side in range(len(includes)):
            queries = slice_channels(near_rows[0, near_side], column, block_width).reshape(
                shape_rows
            )
            cotangent = slice_channels(near_rows[1, near_side], column, block_width).reshape(
                shape_rows
            )
            block_stats = lax.dynamic_slice_in_dim(
                near_stats[:, near_side], head_start, heads_block, 2
            )
            visible = includes[near_side][:, None, None, None]
            scores = (
                jnp.einsum(
                    "tqhd,tkhd->thqk", queries, keys_block, preferred_element_type=jnp.float32
                )
                * softmax_scale
            )
            safe_sum = jnp.where(visible, block_stats[1][..., None], 1.0)
            weights = jnp.where(
                visible, jnp.exp(scores - block_stats[0][..., None]) / safe_sum, 0.0
            )
            weights_low = weights.astype(jnp.bfloat16)
            dweights = jnp.einsum(
                "tqhd,tkhd->thqk", cotangent, values_block, preferred_element_type=jnp.float32
            )
            dscores = (weights * (dweights - block_stats[2][..., None]) * softmax_scale).astype(
                jnp.bfloat16
            )
            key_sum = key_sum + jnp.einsum(
                "thqk,tqhd->tkhd", dscores, queries, preferred_element_type=jnp.float32
            )
            value_sum = value_sum + jnp.einsum(
                "thqk,tqhd->tkhd", weights_low, cotangent, preferred_element_type=jnp.float32
            )
        key_total = lax.dynamic_update_slice_in_dim(
            key_total,
            slice_channels(key_total, column, block_width)
            + key_sum.reshape(tokens_here, block_width),
            column,
            1,
        )
        value_total = lax.dynamic_update_slice_in_dim(
            value_total,
            slice_channels(value_total, column, block_width)
            + value_sum.reshape(tokens_here, block_width),
            column,
            1,
        )
        return (key_total, value_total)

    key_total, value_total = lax.fori_loop(
        0, block_count, neighbour_block_step, (key_start, value_start)
    )
    return (key_total.astype(jnp.bfloat16), value_total.astype(jnp.bfloat16))


def shards(query_rows, key_rows, value_rows, out_cotangent, tile_slot, window_reach):
    tokens_here, channels = query_rows.shape
    tm_count = lax.axis_size("tm")
    space_count = lax.axis_size("space")
    per_peer = tokens_here // (tm_count * space_count)
    own_rank = lax.axis_index("tm") * space_count + lax.axis_index("space")
    landing = tile_slot // tokens_here * per_peer + tile_slot % tokens_here - own_rank * per_peer
    chosen = (
        jnp.zeros((tokens_here,), jnp.int32)
        .at[landing]
        .set(jnp.arange(tokens_here, dtype=jnp.int32))
    )
    send_query = query_rows[chosen]
    send_key = key_rows[chosen]
    send_value = value_rows[chosen]
    send_grad = out_cotangent[chosen]
    query_tile, key_tile, value_tile, grad_tile = (
        lax.all_to_all(send_query, ("tm", "space"), split_axis=0, concat_axis=0, tiled=True),
        lax.all_to_all(send_key, ("tm", "space"), split_axis=0, concat_axis=0, tiled=True),
        lax.all_to_all(send_value, ("tm", "space"), split_axis=0, concat_axis=0, tiled=True),
        lax.all_to_all(send_grad, ("tm", "space"), split_axis=0, concat_axis=0, tiled=True),
    )
    tiles_here = tokens_here // TILE
    slab_index = lax.axis_index("tm")
    column_count = space_count * tiles_here
    column_ids = lax.axis_index("space") * tiles_here + jnp.arange(tiles_here, dtype=jnp.int32)
    left_open = column_ids > 0
    right_open = column_ids < column_count - 1
    own_reach = lax.dynamic_index_in_dim(window_reach, slab_index, 0, keepdims=False)
    allowed = jnp.stack(
        [own_reach[:, 0] > 0, own_reach[:, 0] >= 0, own_reach[:, 1] > 0, left_open, right_open],
        axis=1,
    )
    tile_grid = (1, tiles_here, TILE, channels)
    stacked_pair = jnp.stack([key_tile.reshape(tile_grid), value_tile.reshape(tile_grid)])
    extended = extended_2(stacked_pair, (("tm", 1), ("space", 2)), 1)
    near_pair = five_sets(extended).reshape(2, 5, tokens_here, channels)
    keep_range = (0, 3)
    attended_tile, query_grad_tile, key_terms, value_terms, row_stats = attend_all(
        query_tile, grad_tile, near_pair[0], near_pair[1], allowed, keep_range
    )
    column_stats = extended_2(row_stats, (("space", 1),), 1)
    left_stats = column_stats[:, :-2]
    right_stats = column_stats[:, 2:]
    lower_terms = passed_along(jnp.stack([key_terms[0], value_terms[0]]), "tm", -1)
    upper_terms = passed_along(jnp.stack([key_terms[2], value_terms[2]]), "tm", 1)
    key_start = key_terms[1] + lower_terms[0] + upper_terms[0]
    value_start = value_terms[1] + lower_terms[1] + upper_terms[1]
    stacked_rows = jnp.stack(
        [
            query_tile.reshape(tiles_here, TILE, channels),
            grad_tile.reshape(tiles_here, TILE, channels),
        ]
    )
    side_halo = extended_2(stacked_rows, (("space", 1),), 1)
    side_rows = jnp.stack([side_halo[:, :-2], side_halo[:, 2:]], axis=1).reshape(
        2, 2, tokens_here, channels
    )
    side_stats = jnp.stack([left_stats, right_stats], axis=1)
    key_grad_tile, value_grad_tile = neighbour_terms(
        side_rows, side_stats, key_tile, value_tile, (left_open, right_open), key_start, value_start
    )
    back_rows = (
        lax.all_to_all(attended_tile, ("tm", "space"), split_axis=0, concat_axis=0, tiled=True),
        lax.all_to_all(query_grad_tile, ("tm", "space"), split_axis=0, concat_axis=0, tiled=True),
        lax.all_to_all(key_grad_tile, ("tm", "space"), split_axis=0, concat_axis=0, tiled=True),
        lax.all_to_all(value_grad_tile, ("tm", "space"), split_axis=0, concat_axis=0, tiled=True),
    )
    return (
        back_rows[0][landing],
        back_rows[1][landing],
        back_rows[2][landing],
        back_rows[3][landing],
    )


def solution(mesh):
    return jax.shard_map(
        shards,
        mesh=mesh,
        in_specs=(
            P(("tm", "space"), None),
            P(("tm", "space"), None),
            P(("tm", "space"), None),
            P(("tm", "space"), None),
            P(("tm", "space")),
            P(None, "space", None),
        ),
        out_specs=(
            P(("tm", "space"), None),
            P(("tm", "space"), None),
            P(("tm", "space"), None),
            P(("tm", "space"), None),
        ),
        check_vma=False,
    )
```

profile of v0, /device:TPU:1, one launch (start us, length us, event | category | flops | bytes accessed | tf_op | source)
XLA Modules:
  0.0 874.0 jit_solution(1871915619202582587)
XLA Ops:
  5.7 11.5 %all-to-all-start = ((bf16[128,2,2560]{2,1,0:T(2,128)(2,1)}), bf16[128,2,2560]{2,1,0:T(2,128)(2,1)S(1)}, u32[]{:S(2)}, u32[]{:S(2)}) async-start(bf16[128,2,2560]{2,1,0:T(2,128)(2,1)} %all_to_all.64), calls=%async_computation | async-start | bytes 2621440 | tf_op jit(solution)/shard_map/all_to_all | solution.py:223
  23.7 15.2 %all-to-all-done = bf16[128,2,2560]{2,1,0:T(2,128)(2,1)S(1)} async-done(((bf16[128,2,2560]{2,1,0:T(2,128)(2,1)}), bf16[128,2,2560]{2,1,0:T(2,128)(2,1)S(1)}, u32[]{:S(2)}, u32[]{:S(2)}) %all-to-all-start) | async-done | bytes 1310752 | tf_op jit(solution)/shard_map/all_to_all | solution.py:223
  47.4 17.9 %all-to-all-done.1 = bf16[128,2,2560]{2,1,0:T(2,128)(2,1)S(1)} async-done(((bf16[128,2,2560]{2,1,0:T(2,128)(2,1)}), bf16[128,2,2560]{2,1,0:T(2,128)(2,1)S(1)}, u32[]{:S(2)}, u32[]{:S(2)}) %all-to-all-start.1) | async-done | bytes 1310752 | tf_op jit(solution)/shard_map/all_to_all | solution.py:224
  73.0 111.2 %collective-permute-done = bf16[2,1,1,256,2560]{4,3,2,1,0:T(8,128)(2,1)S(1)} collective-permute-done((bf16[2,1,1,256,2560]{4,3,2,1,0:T(8,128)(2,1)}, bf16[2,1,1,256,2560]{4,3,2,1,0:T(8,128)(2,1)S(1)}, u32[]{:S(2)}, u32[]{:S(2)}) %collective-permute-start) | collective-permute-done | bytes 2621472 | tf_op jit(solution)/shard_map/ppermute | solution.py:19
  184.2 5.8 collective-permute-done.1
  190.0 6.1 pad_maximum_fusion
  216.4 91.6 %all-to-all-done.2 = bf16[128,2,2560]{2,1,0:T(2,128)(2,1)S(1)} async-done(((bf16[128,2,2560]{2,1,0:T(2,128)(2,1)}), bf16[128,2,2560]{2,1,0:T(2,128)(2,1)S(1)}, u32[]{:S(2)}, u32[]{:S(2)}) %all-to-all-start.2) | async-done | bytes 1310752 | tf_op jit(solution)/shard_map/all_to_all | solution.py:222
  308.0 10.3 %all-to-all-start.3 = ((bf16[128,2,2560]{2,1,0:T(2,128)(2,1)}), bf16[128,2,2560]{2,1,0:T(2,128)(2,1)S(1)}, u32[]{:S(2)}, u32[]{:S(2)}) async-start(bf16[128,2,2560]{2,1,0:T(2,128)(2,1)} %all_to_all.71), calls=%async_computation.3 | async-start | bytes 2621440 | tf_op jit(solution)/shard_map/all_to_all | solution.py:225
  322.5 17.4 %all-to-all-done.3 = bf16[128,2,2560]{2,1,0:T(2,128)(2,1)S(1)} async-done(((bf16[128,2,2560]{2,1,0:T(2,128)(2,1)}), bf16[128,2,2560]{2,1,0:T(2,128)(2,1)S(1)}, u32[]{:S(2)}, u32[]{:S(2)}) %all-to-all-start.3) | async-done | bytes 1310752 | tf_op jit(solution)/shard_map/all_to_all | solution.py:225
  364.6 166.0 %while.36 = (s32[]{:T(128)}, bf16[256,2560]{1,0:T(8,128)(2,1)}, bf16[256,2560]{1,0:T(8,128)(2,1)}, f32[3,256,2560]{1,2,0:T(8,128)}, f32[3,256,2560]{1,2,0:T(8,12...) while((s32[]{:T(128)}, bf16[256,2560]{1,0:T(8,128)(2,1)}, ...), condition=%wide.region_5.6_spmd, body=%wide.region_1.5_spmd.sunk | while | flops 2217414400 | bytes 175089072 | solution.py:131
  555.8 5.5 collective-permute-start.6
  565.6 6.0 all-to-all-start.4
  571.7 56.8 %collective-permute-done.7 = bf16[2,1,256,2560]{3,2,1,0:T(8,128)(2,1)} collective-permute-done((bf16[2,1,256,2560]{3,2,1,0:T(8,128)(2,1)}, bf16[2,1,256,2560]{3,2,1,0:T(8,128)(2,1)}, u32[]{:S(2)}, u32[]{:S(2)}) %collective-permute-start.7) | collective-permute-done | bytes 2621472 | tf_op jit(solution)/shard_map/ppermute | solution.py:21
  628.4 5.4 maximum_bitcast_fusion.1
  633.9 8.1 copy.124
  647.2 26.0 %collective-permute-done.5 = f32[2,256,2560]{1,2,0:T(8,128)} collective-permute-done((f32[2,256,2560]{1,2,0:T(8,128)}, f32[2,256,2560]{1,2,0:T(8,128)}, u32[]{:S(2)}, u32[]{:S(2)}) %collective-permute-start.5) | collective-permute-done | bytes 5242912 | tf_op jit(solution)/shard_map/ppermute | solution.py:31
  673.2 8.3 collective-permute-done.4
  681.6 9.0 %fusion.55 = (f32[256,2560]{0,1:T(8,128)}, f32[256,2560]{0,1:T(8,128)}) fusion(f32[2,256,2560]{1,2,0:T(8,128)} %collective-permute-done.5, f32[2,256,2560]{1,2,0:T(8,128)} %collective-permute-done.4, f32[3,256,2560]{1,2,0:T(8,128)} %get-tuple-element.365, f32[3,256,2560]{1,2,0:T(8,128)} %get-tuple-element.364), kind=kLoop, calls=%fused_computation.99 | loop fusion | flops 2621440 | bytes 20971520 | tf_op jit(solution)/shard_map/add | solution.py:252
  690.5 25.2 %all-to-all-start.5 = ((bf16[128,2,2560]{2,1,0:T(2,128)(2,1)}), bf16[128,2,2560]{2,1,0:T(2,128)(2,1)}, u32[]{:S(2)}, u32[]{:S(2)}) async-start(bf16[128,2,2560]{2,1,0:T(2,128)(2,1)} %all_to_all.77), calls=%async_computation.5 | async-start | bytes 2621440 | tf_op jit(solution)/shard_map/all_to_all | solution.py:269
  715.8 89.3 %while.37 = (s32[]{:T(128)}, f32[256,2560]{0,1:T(8,128)}, f32[256,2560]{0,1:T(8,128)}, bf16[2,2,256,2560]{2,3,1,0:T(8,128)(2,1)}, pred[1]{0:T(512)(128)(4,1)}, /...) while((s32[]{:T(128)}, f32[256,2560]{0,1:T(8,128)}, ...), condition=%wide.region_7.8_spmd, body=%wide.region_6.7_spmd.sunk | while | flops 677644800 | bytes 40724916 | solution.py:199
  809.0 10.1 %all-to-all-start.6 = ((bf16[128,2,2560]{2,1,0:T(2,128)(2,1)}), bf16[128,2,2560]{2,1,0:T(2,128)(2,1)S(1)}, u32[]{:S(2)}, u32[]{:S(2)}) async-start(bf16[128,2,2560]{2,1,0:T(2,128)(2,1)} %all_to_all.82), calls=%async_computation.6 | async-start | bytes 2621440 | tf_op jit(solution)/shard_map/all_to_all | solution.py:270
  826.7 14.0 %all-to-all-done.6 = bf16[128,2,2560]{2,1,0:T(2,128)(2,1)S(1)} async-done(((bf16[128,2,2560]{2,1,0:T(2,128)(2,1)}), bf16[128,2,2560]{2,1,0:T(2,128)(2,1)S(1)}, u32[]{:S(2)}, u32[]{:S(2)}) %all-to-all-start.6) | async-done | bytes 1310752 | tf_op jit(solution)/shard_map/all_to_all | solution.py:270
  840.7 5.7 all-to-all-start.7
  858.2 9.7 %all-to-all-done.7 = bf16[128,2,2560]{2,1,0:T(2,128)(2,1)} async-done(((bf16[128,2,2560]{2,1,0:T(2,128)(2,1)}), bf16[128,2,2560]{2,1,0:T(2,128)(2,1)}, u32[]{:S(2)}, u32[]{:S(2)}) %all-to-all-start.7) | async-done | bytes 1310752 | tf_op jit(solution)/shard_map/all_to_all | solution.py:271
  (368 shorter events, 392.6 us)
Async XLA Ops:
  5.7 33.1 %all-to-all-start = ((bf16[128,2,2560]{2,1,0:T(2,128)(2,1)}), bf16[128,2,2560]{2,1,0:T(2,128)(2,1)S(1)}, u32[]{:S(2)}, u32[]{:S(2)}) async-start(bf16[128,2,2560]{2,1,0:T(2,128)(2,1)} %all_to_all.64), calls=%async_computation | async-start | bytes 2621440 | tf_op jit(solution)/shard_map/all_to_all | solution.py:223
  38.9 26.5 %all-to-all-start.1 = ((bf16[128,2,2560]{2,1,0:T(2,128)(2,1)}), bf16[128,2,2560]{2,1,0:T(2,128)(2,1)S(1)}, u32[]{:S(2)}, u32[]{:S(2)}) async-start(bf16[128,2,2560]{2,1,0:T(2,128)(2,1)} %all_to_all.66), calls=%async_computation.1 | async-start | bytes 2621440 | tf_op jit(solution)/shard_map/all_to_all | solution.py:224
  65.9 130.2 %copy-start.21 = (bf16[1,1,1,256,2560]{4,3,2,1,0:T(8,128)(2,1)}, bf16[1,1,1,256,2560]{4,3,2,1,0:T(8,128)(2,1)S(1)}, u32[]{:S(2)}) copy-start(bf16[1,1,1,256,2560]{4,3,2,1,0:T(8,128)(2,1)S(1)} %stack_reshape.13) | copy-start | bytes 3932164
  67.1 117.1 %collective-permute-start = (bf16[2,1,1,256,2560]{4,3,2,1,0:T(8,128)(2,1)}, bf16[2,1,1,256,2560]{4,3,2,1,0:T(8,128)(2,1)S(1)}, u32[]{:S(2)}, u32[]{:S(2)}) collective-permute-start(bf16[2,1,1,256,2560]{4,3,2,1,0:T(8,128)(2,1)} %constant_dynamic-update-slice_fusion.6), channel_id=1, source_target_pairs={{0,32},{32,64},{64,96},{1,33},{33,65},{65,97},{2,34},{34,66},{66,9... | collective-permute-start | bytes 7864328 | tf_op jit(solution)/shard_map/ppermute | solution.py:19
  71.0 119.0 %collective-permute-start.1 = (bf16[2,1,1,256,2560]{4,3,2,1,0:T(8,128)(2,1)}, bf16[2,1,1,256,2560]{4,3,2,1,0:T(8,128)(2,1)S(1)}, u32[]{:S(2)}, u32[]{:S(2)}) collective-permute-start(bf16[2,1,1,256,2560]{4,3,2,1,0:T(8,128)(2,1)} %constant_dynamic-update-slice_fusion.6), channel_id=1, source_target_pairs={{32,0},{64,32},{96,64},{33,1},{65,33},{97,65},{34,2},{66,34},{98,6... | collective-permute-start | bytes 7864328 | tf_op jit(solution)/shard_map/ppermute | solution.py:21
  196.1 149.8 %collective-permute-start.2 = (bf16[2,3,1,256,2560]{4,3,2,1,0:T(8,128)(2,1)}, bf16[2,3,1,256,2560]{4,3,2,1,0:T(8,128)(2,1)}, u32[]{:S(2)}, u32[]{:S(2)}) collective-permute-start(bf16[2,3,1,256,2560]{4,3,2,1,0:T(8,128)(2,1)} %pad_maximum_fusion), channel_id=1, source_target_pairs={{0,1},{1,2},{2,3},{3,4},{4,5},{5,6},{6,7},{7,8},{8,9},{9,10},{10,1... | collective-permute-start | bytes 23592968 | tf_op jit(solution)/shard_map/ppermute | solution.py:19
  200.5 147.3 %collective-permute-start.3 = (bf16[2,3,1,256,2560]{4,3,2,1,0:T(8,128)(2,1)}, bf16[2,3,1,256,2560]{4,3,2,1,0:T(8,128)(2,1)}, u32[]{:S(2)}, u32[]{:S(2)}) collective-permute-start(bf16[2,3,1,256,2560]{4,3,2,1,0:T(8,128)(2,1)} %pad_maximum_fusion), channel_id=1, source_target_pairs={{1,0},{2,1},{3,2},{4,3},{5,4},{6,5},{7,6},{8,7},{9,8},{10,9},{11,1... | collective-permute-start | bytes 23592968 | tf_op jit(solution)/shard_map/ppermute | solution.py:21
  204.6 103.4 %all-to-all-start.2 = ((bf16[128,2,2560]{2,1,0:T(2,128)(2,1)}), bf16[128,2,2560]{2,1,0:T(2,128)(2,1)S(1)}, u32[]{:S(2)}, u32[]{:S(2)}) async-start(bf16[128,2,2560]{2,1,0:T(2,128)(2,1)} %all_to_all.68), calls=%async_computation.2 | async-start | bytes 2621440 | tf_op jit(solution)/shard_map/all_to_all | solution.py:222
  212.4 105.9 %copy-start.35 = (s32[4,1,2]{0,2,1:T(2,128)S(1)}, s32[4,1,2]{0,2,1:T(2,128)}, u32[]{:S(2)}) copy-start(s32[4,1,2]{0,2,1:T(2,128)} %param.15) | copy-start | bytes 100
  308.0 14.5 %copy-start.16 = (bf16[128,2,2560]{2,1,0:T(2,128)(2,1)}, bf16[128,2,2560]{2,1,0:T(2,128)(2,1)S(1)}, u32[]{:S(2)}) copy-start(bf16[128,2,2560]{2,1,0:T(2,128)(2,1)S(1)} %all-to-all-done.2) | copy-start | bytes 3932164
  308.0 32.0 %all-to-all-start.3 = ((bf16[128,2,2560]{2,1,0:T(2,128)(2,1)}), bf16[128,2,2560]{2,1,0:T(2,128)(2,1)S(1)}, u32[]{:S(2)}, u32[]{:S(2)}) async-start(bf16[128,2,2560]{2,1,0:T(2,128)(2,1)} %all_to_all.71), calls=%async_computation.3 | async-start | bytes 2621440 | tf_op jit(solution)/shard_map/all_to_all | solution.py:225
  538.2 135.0 %collective-permute-start.5 = (f32[2,256,2560]{1,2,0:T(8,128)}, f32[2,256,2560]{1,2,0:T(8,128)}, u32[]{:S(2)}, u32[]{:S(2)}) collective-permute-start(f32[2,256,2560]{1,2,0:T(8,128)} %pad_maximum_fusion.2), channel_id=1, source_target_pairs={{0,32},{32,64},{64,96},{1,33},{33,65},{65,97},{2,34},{34,66},{66,9... | collective-permute-start | bytes 15728648 | tf_op jit(solution)/shard_map/ppermute | solution.py:31
  544.7 136.8 %collective-permute-start.4 = (f32[2,256,2560]{1,2,0:T(8,128)}, f32[2,256,2560]{1,2,0:T(8,128)}, u32[]{:S(2)}, u32[]{:S(2)}) collective-permute-start(f32[2,256,2560]{1,2,0:T(8,128)} %pad_maximum_fusion.1), channel_id=1, source_target_pairs={{32,0},{64,32},{96,64},{33,1},{65,33},{97,65},{34,2},{66,34},{98,6... | collective-permute-start | bytes 15728648 | tf_op jit(solution)/shard_map/ppermute | solution.py:31
  554.5 74.0 %collective-permute-start.7 = (bf16[2,1,256,2560]{3,2,1,0:T(8,128)(2,1)}, bf16[2,1,256,2560]{3,2,1,0:T(8,128)(2,1)}, u32[]{:S(2)}, u32[]{:S(2)}) collective-permute-start(bf16[2,1,256,2560]{3,2,1,0:T(8,128)(2,1)} %constant_dynamic-update-slice_fusion.12), channel_id=1, source_target_pairs={{1,0},{2,1},{3,2},{4,3},{5,4},{6,5},{7,6},{8,7},{9,8},{10,9},{11,1... | collective-permute-start | bytes 7864328 | tf_op jit(solution)/shard_map/ppermute | solution.py:21
  555.8 72.7 %collective-permute-start.6 = (bf16[2,1,256,2560]{3,2,0,1:T(8,128)(2,1)}, bf16[2,1,256,2560]{3,2,0,1:T(8,128)(2,1)}, u32[]{:S(2)}, u32[]{:S(2)}) collective-permute-start(bf16[2,1,256,2560]{3,2,0,1:T(8,128)(2,1)} %bitcast.60), channel_id=1, source_target_pairs={{0,1},{1,2},{2,3},{3,4},{4,5},{5,6},{6,7},{7,8},{8,9},{9,10},{10,1... | collective-permute-start | bytes 7864328 | tf_op jit(solution)/shard_map/ppermute | solution.py:19
  565.6 124.9 %all-to-all-start.4 = ((bf16[128,2,2560]{2,1,0:T(2,128)(2,1)}), bf16[128,2,2560]{2,1,0:T(2,128)(2,1)S(1)}, u32[]{:S(2)}, u32[]{:S(2)}) async-start(bf16[128,2,2560]{2,1,0:T(2,128)(2,1)} %all_to_all.74), calls=%async_computation.4 | async-start | bytes 2621440 | tf_op jit(solution)/shard_map/all_to_all | solution.py:268
  642.0 73.8 %collective-permute-start.8 = (f32[3,1,20,256]{3,2,1,0:T(8,128)S(1)}, f32[3,1,20,256]{3,2,1,0:T(8,128)S(1)}, u32[]{:S(2)}, u32[]{:S(2)}) collective-permute-start(f32[3,1,20,256]{3,2,1,0:T(8,128)S(1)} %bitcast.267), channel_id=1, source_target_pairs={{0,1},{1,2},{2,3},{3,4},{4,5},{5,6},{6,7},{7,8},{8,9},{9,10},{10,1... | collective-permute-start | bytes 184328 | tf_op jit(solution)/shard_map/ppermute | solution.py:19
  644.5 71.2 %collective-permute-start.9 = (f32[3,1,20,256]{3,2,1,0:T(8,128)S(1)}, f32[3,1,20,256]{3,2,1,0:T(8,128)S(1)}, u32[]{:S(2)}, u32[]{:S(2)}) collective-permute-start(f32[3,1,20,256]{3,2,1,0:T(8,128)S(1)} %bitcast.268), channel_id=1, source_target_pairs={{1,0},{2,1},{3,2},{4,3},{5,4},{6,5},{7,6},{8,7},{9,8},{10,9},{11,1... | collective-permute-start | bytes 184328 | tf_op jit(solution)/shard_map/ppermute | solution.py:21
  690.5 25.2 %copy-start.26 = (bf16[128,2,2560]{2,1,0:T(2,128)(2,1)}, bf16[128,2,2560]{2,1,0:T(2,128)(2,1)S(1)}, u32[]{:S(2)}) copy-start(bf16[128,2,2560]{2,1,0:T(2,128)(2,1)S(1)} %all-to-all-done.4) | copy-start | bytes 3932164
  690.5 118.5 %all-to-all-start.5 = ((bf16[128,2,2560]{2,1,0:T(2,128)(2,1)}), bf16[128,2,2560]{2,1,0:T(2,128)(2,1)}, u32[]{:S(2)}, u32[]{:S(2)}) async-start(bf16[128,2,2560]{2,1,0:T(2,128)(2,1)} %all_to_all.77), calls=%async_computation.5 | async-start | bytes 2621440 | tf_op jit(solution)/shard_map/all_to_all | solution.py:269
  809.0 31.6 %all-to-all-start.6 = ((bf16[128,2,2560]{2,1,0:T(2,128)(2,1)}), bf16[128,2,2560]{2,1,0:T(2,128)(2,1)S(1)}, u32[]{:S(2)}, u32[]{:S(2)}) async-start(bf16[128,2,2560]{2,1,0:T(2,128)(2,1)} %all_to_all.82), calls=%async_computation.6 | async-start | bytes 2621440 | tf_op jit(solution)/shard_map/all_to_all | solution.py:270
  822.6 23.8 %copy-start.34 = (s32[256]{0:T(256)S(1)}, s32[256]{0:T(256)}, u32[]{:S(2)}) copy-start(s32[256]{0:T(256)} %copy-done.33) | copy-start | bytes 3076
  822.6 23.8 %copy-start.27 = (bf16[128,2,2560]{2,1,0:T(2,128)(2,1)S(1)}, bf16[128,2,2560]{2,1,0:T(2,128)(2,1)}, u32[]{:S(2)}) copy-start(bf16[128,2,2560]{2,1,0:T(2,128)(2,1)} %copy-done.26) | copy-start | bytes 3932164
  840.7 27.2 %all-to-all-start.7 = ((bf16[128,2,2560]{2,1,0:T(2,128)(2,1)}), bf16[128,2,2560]{2,1,0:T(2,128)(2,1)}, u32[]{:S(2)}, u32[]{:S(2)}) async-start(bf16[128,2,2560]{2,1,0:T(2,128)(2,1)} %all_to_all.85), calls=%async_computation.7 | async-start | bytes 2621440 | tf_op jit(solution)/shard_map/all_to_all | solution.py:271
  (59 other events, 253.2 us)
where the time goes:
time: 886 us; the launch traced here: 874 us
  waiting for transfers between devices  374 us (42%)
  local copies, waits for them, and re-layouts  230 us (26%)
  starting transfers between devices  108 us (12%)
  matrix products  89.5 us (10%)
  other arithmetic  68.1 us (8%)
    ppermute x4, waiting for transfers between devices, extended_2(): lax.ppermute(tail, axis, [(i, (i + 1) % count) for i in range(ends)])  111 us
    all_to_all x1, waiting for transfers between devices, shards(): lax.all_to_all(send_query, ('tm', 'space'), split_axis=0, concat_axis=0,...  91.6 us
    dynamic_slice x52, local copies, waits for them, and re-layouts, slice_channels(): return lax.dynamic_slice_in_dim(array, column, block_width, array.ndim - 1)  78 us
    ppermute x4, waiting for transfers between devices, extended_2(): lax.ppermute(head, axis, [((i + 1) % count, i) for i in range(ends)])  62.6 us
    ppermute x2, waiting for transfers between devices, passed_along(): return lax.ppermute(block, axis, route)  34.3 us
    all_to_all x1, starting transfers between devices, shards(): lax.all_to_all(query_grad_tile, ('tm', 'space'), split_axis=0, concat_axi...  25.2 us
    dot_general x4, matrix products, attend_block_step(): jnp.einsum('tqhd,atkhd->thqak', cotangent, values_block, preferred_elemen...  20.6 us
    dot_general x8, matrix products, neighbour_block_step(): jnp.einsum('thqk,tqhd->tkhd', dscores, queries, preferred_element_type=jn...  20.2 us
  transfers between devices with their start and end apart: 18, of which 11 were waited for; matrix products, arithmetic and copies ran while one was open for 17% of the time, Pallas kernels for 0%

commit v1 on v0

v1 whole, which is shorter than its diff:
```python
import functools

import jax
import jax.numpy as jnp
from jax import lax
from jax.experimental import pallas as pl
from jax.experimental.pallas import tpu as pltpu
from jax.sharding import PartitionSpec as P

H = 20
HD = 128
TILE = 256
SETS = 5
NT_DIMS = (((1,), (1,)), ((), ()))


def _attn_kernel(flags_ref, q_ref, g_ref, k_ref, v_ref, kb_ref, ka_ref, kl_ref, kr_ref,
                 o_ref, dq_ref, dko_ref, dvo_ref, nb_b, nb_a, nb_l, nb_r, s_scr, dp_scr):
    scale = HD ** (-0.5)
    q = q_ref[...]
    g = g_ref[...]
    keys = [kb_ref[0], k_ref[...], ka_ref[0], kl_ref[0], kr_ref[0]]
    vals = [kb_ref[1], v_ref[...], ka_ref[1], kl_ref[1], kr_ref[1]]
    nb_out = [nb_b, None, nb_a, nb_l, nb_r]
    vis = [flags_ref[a] > 0 for a in range(SETS)]

    m = jnp.full((TILE, 1), -1e30, jnp.float32)
    for a in range(SETS):
        s = lax.dot_general(q, keys[a], NT_DIMS, preferred_element_type=jnp.float32) * scale
        s = jnp.where(vis[a], s, -1e30)
        s_scr[a] = s
        m = jnp.maximum(m, jnp.max(s, axis=1, keepdims=True))
    l = jnp.zeros((TILE, 1), jnp.float32)
    for a in range(SETS):
        e = jnp.where(vis[a], jnp.exp(s_scr[a] - m), 0.0)
        s_scr[a] = e
        l = l + jnp.sum(e, axis=1, keepdims=True)
    inv = 1.0 / l
    o = jnp.zeros((TILE, HD), jnp.float32)
    rd = jnp.zeros((TILE, 1), jnp.float32)
    for a in range(SETS):
        p = s_scr[a] * inv
        pb = p.astype(jnp.bfloat16)
        o = o + jnp.dot(pb, vals[a], preferred_element_type=jnp.float32)
        dp = lax.dot_general(g, vals[a], NT_DIMS, preferred_element_type=jnp.float32)
        rd = rd + jnp.sum(p * dp, axis=1, keepdims=True)
        s_scr[a] = p
        dp_scr[a] = dp
        dv = jnp.dot(p.T.astype(jnp.bfloat16), g, preferred_element_type=jnp.float32)
        if a == 1:
            dvo_ref[...] = dv
        else:
            nb_out[a][1] = dv.astype(jnp.bfloat16)
    o_ref[...] = o.astype(jnp.bfloat16)
    dq = jnp.zeros((TILE, HD), jnp.float32)
    for a in range(SETS):
        ds = s_scr[a] * (dp_scr[a] - rd) * scale
        dq = dq + jnp.dot(ds.astype(jnp.bfloat16), keys[a], preferred_element_type=jnp.float32)
        dk = jnp.dot(ds.T.astype(jnp.bfloat16), q, preferred_element_type=jnp.float32)
        if a == 1:
            dko_ref[...] = dk
        else:
            nb_out[a][0] = dk.astype(jnp.bfloat16)
    dq_ref[...] = dq.astype(jnp.bfloat16)


def attend_tile(flags, recv, kv_below, kv_above, kv_left, kv_right):
    tokens = recv.shape[0]
    own = lambda part: pl.BlockSpec((tokens, HD), lambda h, f, part=part: (0, part * H + h))
    pair = pl.BlockSpec((2, tokens, HD), lambda h, f: (0, 0, h))
    head = pl.BlockSpec((tokens, HD), lambda h, f: (0, h))
    flops = 6 * SETS * 2 * tokens * TILE * HD * H
    bytes_accessed = (4 * 2 + 4 * 4 + 4 * 2 * 2 + 2 * 2 + 2 * 4 + 4 * 2 * 2) * tokens * HD * H
    out_shape = (
        jax.ShapeDtypeStruct((tokens, H * HD), jnp.bfloat16),
        jax.ShapeDtypeStruct((tokens, H * HD), jnp.bfloat16),
        jax.ShapeDtypeStruct((tokens, H * HD), jnp.float32),
        jax.ShapeDtypeStruct((tokens, H * HD), jnp.float32),
    ) + tuple(jax.ShapeDtypeStruct((2, tokens, H * HD), jnp.bfloat16) for _ in range(4))
    return pl.pallas_call(
        _attn_kernel,
        out_shape=out_shape,
        grid_spec=pltpu.PrefetchScalarGridSpec(
            num_scalar_prefetch=1,
            grid=(H,),
            in_specs=[own(0), own(3), own(1), own(2), pair, pair, pair, pair],
            out_specs=[head, head, head, head, pair, pair, pair, pair],
            scratch_shapes=[
                pltpu.VMEM((SETS, tokens, TILE), jnp.float32),
                pltpu.VMEM((SETS, tokens, TILE), jnp.float32),
            ],
        ),
        compiler_params=pltpu.CompilerParams(dimension_semantics=("arbitrary",)),
        cost_estimate=pl.CostEstimate(
            flops=flops, transcendentals=SETS * tokens * TILE * H, bytes_accessed=bytes_accessed
        ),
    )(flags, recv, recv, recv, recv, kv_below, kv_above, kv_left, kv_right)


def shifted(block, axis, distance):
    devices = range(lax.axis_size(axis))
    route = [(i - distance, i) for i in devices if i - distance in devices]
    return lax.ppermute(block, axis, route)


def shards(query_rows, key_rows, value_rows, out_cotangent, tile_slot, window_reach):
    tokens_here, channels = query_rows.shape
    tm_count = lax.axis_size("tm")
    space_count = lax.axis_size("space")
    per_peer = tokens_here // (tm_count * space_count)
    own_rank = lax.axis_index("tm") * space_count + lax.axis_index("space")
    landing = tile_slot // tokens_here * per_peer + tile_slot % tokens_here - own_rank * per_peer
    chosen = (
        jnp.zeros((tokens_here,), jnp.int32)
        .at[landing]
        .set(jnp.arange(tokens_here, dtype=jnp.int32))
    )
    send = jnp.concatenate(
        [query_rows[chosen], key_rows[chosen], value_rows[chosen], out_cotangent[chosen]], axis=1
    )
    recv = lax.all_to_all(send, ("tm", "space"), split_axis=0, concat_axis=0, tiled=True)
    slab_index = lax.axis_index("tm")
    column = lax.axis_index("space")
    own_reach = lax.dynamic_index_in_dim(window_reach, slab_index, 0, keepdims=False)[0]
    flags = jnp.stack(
        [own_reach[0] > 0, own_reach[0] >= 0, own_reach[1] > 0, column > 0, column < space_count - 1]
    ).astype(jnp.int32)
    kv_own = jnp.stack([recv[:, channels:2 * channels], recv[:, 2 * channels:3 * channels]])
    kv_below = shifted(kv_own, "tm", 1)
    kv_above = shifted(kv_own, "tm", -1)
    kv_left = shifted(kv_own, "space", 1)
    kv_right = shifted(kv_own, "space", -1)
    attended, query_grad, key_own, value_own, nb_b, nb_a, nb_l, nb_r = attend_tile(
        flags, recv, kv_below, kv_above, kv_left, kv_right
    )
    from_above = shifted(nb_b, "tm", -1)
    from_below = shifted(nb_a, "tm", 1)
    from_right = shifted(nb_l, "space", -1)
    from_left = shifted(nb_r, "space", 1)
    terms = (
        from_above.astype(jnp.float32)
        + from_below.astype(jnp.float32)
        + from_right.astype(jnp.float32)
        + from_left.astype(jnp.float32)
    )
    key_grad = (key_own + terms[0]).astype(jnp.bfloat16)
    value_grad = (value_own + terms[1]).astype(jnp.bfloat16)
    out_tile = jnp.concatenate([attended, query_grad, key_grad, value_grad], axis=1)
    back = lax.all_to_all(out_tile, ("tm", "space"), split_axis=0, concat_axis=0, tiled=True)
    rows = back[landing]
    return tuple(rows[:, i * channels:(i + 1) * channels] for i in range(4))


def solution(mesh):
    return jax.shard_map(
        shards,
        mesh=mesh,
        in_specs=(
            P(("tm", "space"), None),
            P(("tm", "space"), None),
            P(("tm", "space"), None),
            P(("tm", "space"), None),
            P(("tm", "space")),
            P(None, "space", None),
        ),
        out_specs=(
            P(("tm", "space"), None),
            P(("tm", "space"), None),
            P(("tm", "space"), None),
            P(("tm", "space"), None),
        ),
        check_vma=False,
    )
```

time: 886 us -> 461 us (0.52); the launches traced: 874 us -> 458 us
  local copies, waits for them, and re-layouts: 230 us -> 66.1 us
  waiting for transfers between devices: 374 us -> 223 us
  matrix products: 89.5 us -> 0 us
  blocking collectives: 0 us -> 76 us
  starting transfers between devices: 108 us -> 32.3 us
  other arithmetic: 68.1 us -> 14.2 us
  Pallas kernels: 0 us -> 43.9 us
    all_to_all x8 -> x1, waiting for transfers between devices: 166 us -> 64 us  [shards(): lax.all_to_all(out_tile, ('tm', 'space'), split_axis=0, concat_axis=0, ti...]
    dot_general x48 -> x0, matrix products: 89.5 us -> none  [the longest x4 20.6 us: attend_block_step(): jnp.einsum('tqhd,atkhd->thqak', cotangent, values_block, preferred_elemen...]
    dynamic_slice x53 -> x1, local copies, waits for them, and re-layouts: 78.1 us -> 0.08 us  [shards(): lax.dynamic_index_in_dim(window_reach, slab_index, 0, keepdims=False)[0]]
    all_to_all x0 -> x1, blocking collectives: none -> 76 us  [shards(): lax.all_to_all(send, ('tm', 'space'), split_axis=0, concat_axis=0, tiled=...]
    all_to_all x8 -> x1, starting transfers between devices: 78.9 us -> 8.27 us  [shards(): lax.all_to_all(out_tile, ('tm', 'space'), split_axis=0, concat_axis=0, ti...]
    ppermute x10 -> x8, waiting for transfers between devices: 208 us -> 159 us  [shifted(): return lax.ppermute(block, axis, route)]
    pallas_call x0 -> x1, Pallas kernels: none -> 43.9 us  [attend_tile(): pl.pallas_call(_attn_kernel, out_shape=out_shape, grid_spec=pltpu.Prefetc...]
    while x73 -> x0, local copies, waits for them, and re-layouts: 25.5 us -> none
  transfers between devices with their start and end apart: 18 -> 9, of which waited for: 11 -> 5; matrix products, arithmetic and copies ran while one was open for 17% -> 0% of each run, Pallas kernels for 0% -> 0%
where the time goes in v1:
time: 461 us; the launch traced here: 458 us
  waiting for transfers between devices  223 us (48%)
  blocking collectives  76 us (16%)
  local copies, waits for them, and re-layouts  66.1 us (14%)
  Pallas kernels  43.9 us (10%)
  starting transfers between devices  32.3 us (7%)
  other arithmetic  14.2 us (3%)
    ppermute x8, waiting for transfers between devices, shifted(): return lax.ppermute(block, axis, route)  159 us
    all_to_all x1, blocking collectives, shards(): lax.all_to_all(send, ('tm', 'space'), split_axis=0, concat_axis=0, tiled=...  76 us
    all_to_all x1, waiting for transfers between devices, shards(): lax.all_to_all(out_tile, ('tm', 'space'), split_axis=0, concat_axis=0, ti...  64 us
    pallas_call x1, Pallas kernels, attend_tile(): pl.pallas_call(_attn_kernel, out_shape=out_shape, grid_spec=pltpu.Prefetc...  43.9 us
    ppermute x8, starting transfers between devices, shifted(): return lax.ppermute(block, axis, route)  24.1 us
    all_to_all x2, local copies, waits for them, and re-layouts, shards(): lax.all_to_all(send, ('tm', 'space'), split_axis=0, concat_axis=0, tiled=...  16.3 us
    all_to_all x2, local copies, waits for them, and re-layouts, shards(): lax.all_to_all(out_tile, ('tm', 'space'), split_axis=0, concat_axis=0, ti...  16.3 us
    gather x1, local copies, waits for them, and re-layouts, shards(): rows = back[landing]  14 us
  transfers between devices with their start and end apart: 9, of which 5 were waited for; matrix products, arithmetic and copies ran while one was open for 0% of the time, Pallas kernels for 0%

profile of v1, /device:TPU:1, one launch (start us, length us, event | category | flops | bytes accessed | tf_op | source)
XLA Modules:
  0.0 458.5 jit_solution(1310452954797118797)
XLA Ops:
  2.9 2.5 gather_fusion
  5.4 2.5 gather_fusion.1
  7.9 2.5 gather_fusion.2
  10.4 2.5 gather_fusion.3
  12.9 5.1 %pad_maximum_fusion = bf16[256,10240]{1,0:T(8,128)(2,1)} fusion(bf16[256,2560]{1,0:T(8,128)(2,1)} %gather_fusion.3, bf16[256,2560]{1,0:T(8,128)(2,1)} %gather_fusion.2, bf16[256,2560]{1,0:T(8,128)(2,1)} %gather_fusion.1, bf16[256,2560]{1,0:T(8,128)(2,1)S(1)} %copy-done.5), kind=kLoop, calls=%fused_computation.6 | loop fusion | flops 20971520 | bytes 10485760 | tf_op jit(solution)/shard_map/concatenate | solution.py:118
  18.0 8.4 %all_to_all.15 = bf16[128,2,10240]{2,1,0:T(2,128)(2,1)} reshape(bf16[256,10240]{1,0:T(8,128)(2,1)} %pad_maximum_fusion) | data formatting | bytes 10485760 | tf_op jit(solution)/shard_map/all_to_all | solution.py:121
  26.4 76.0 %all_to_all.23 = bf16[128,2,10240]{2,1,0:T(2,128)(2,1)} all-to-all(bf16[128,2,10240]{2,1,0:T(2,128)(2,1)} %all_to_all.15), channel_id=1, replica_groups=mesh['tm'=4,'space'=32] {'tm','space'}, dimensions={0} | all-to-all | bytes 10485760 | tf_op jit(solution)/shard_map/all_to_all | solution.py:121
  102.4 7.9 %all_to_all.17.q_ref.g_ref.k_ref.v_ref = bf16[256,10240]{1,0:T(8,128)(2,1)} reshape(bf16[128,2,10240]{2,1,0:T(2,128)(2,1)} %all_to_all.23) | data formatting | bytes 10485760 | tf_op jit(solution)/shard_map/all_to_all | solution.py:121
  113.9 3.3 collective-permute-start
  117.3 3.1 collective-permute-start.1
  120.3 3.4 collective-permute-start.2
  128.2 74.1 %collective-permute-done.kb_ref = bf16[2,256,2560]{2,1,0:T(8,128)(2,1)} collective-permute-done((bf16[2,256,2560]{2,1,0:T(8,128)(2,1)}, bf16[2,256,2560]{2,1,0:T(8,128)(2,1)}, u32[]{:S(2)}, u32[]{:S(2)}) %collective-permute-start) | collective-permute-done | bytes 2621472 | tf_op jit(solution)/shard_map/ppermute | solution.py:103
  202.3 5.9 %collective-permute-done.1.ka_ref = bf16[2,256,2560]{2,1,0:T(8,128)(2,1)} collective-permute-done((bf16[2,256,2560]{2,1,0:T(8,128)(2,1)}, bf16[2,256,2560]{2,1,0:T(8,128)(2,1)}, u32[]{:S(2)}, u32[]{:S(2)}) %collective-permute-start.1) | collective-permute-done | bytes 2621472 | tf_op jit(solution)/shard_map/ppermute | solution.py:103
  208.2 43.9 %shard_map.93 = (bf16[256,2560]{1,0:T(8,128)(2,1)}, bf16[256,2560]{1,0:T(8,128)(2,1)}, f32[256,2560]{1,0:T(8,128)}, f32[256,2560]{1,0:T(8,128)}, bf16[2,256,2560...) custom-call(s32[5]{0:T(128)} %convert_element_type.21.flags_ref, ...), custom_call_target="tpu_custom_call" | custom-call | flops 10066329600 | bytes 44564480 | tf_op jit(solution)/shard_map/pallas_call | solution.py:80
  254.1 5.1 %collective-permute-start.5 = (bf16[2,256,2560]{2,1,0:T(8,128)(2,1)}, bf16[2,256,2560]{2,1,0:T(8,128)(2,1)S(1)}, u32[]{:S(2)}, u32[]{:S(2)}) collective-permute-start(bf16[2,256,2560]{2,1,0:T(8,128)(2,1)} %get-tuple-element.16), channel_id=1, source_target_pairs={{0,32},{32,64},{64,96},{1,33},{33,65},{65,97},{2,34},{34,66},{66,9... | collective-permute-start | bytes 7864328 | tf_op jit(solution)/shard_map/ppermute | solution.py:103
  260.6 4.6 %collective-permute-start.7 = (bf16[2,256,2560]{2,1,0:T(8,128)(2,1)}, bf16[2,256,2560]{2,1,0:T(8,128)(2,1)S(1)}, u32[]{:S(2)}, u32[]{:S(2)}) collective-permute-start(bf16[2,256,2560]{2,1,0:T(8,128)(2,1)} %get-tuple-element.18), channel_id=1, source_target_pairs={{0,1},{1,2},{2,3},{3,4},{4,5},{5,6},{6,7},{7,8},{8,9},{9,10},{10,1... | collective-permute-start | bytes 7864328 | tf_op jit(solution)/shard_map/ppermute | solution.py:103
  265.2 77.9 %collective-permute-done.4 = bf16[2,256,2560]{2,1,0:T(8,128)(2,1)S(1)} collective-permute-done((bf16[2,256,2560]{2,1,0:T(8,128)(2,1)}, bf16[2,256,2560]{2,1,0:T(8,128)(2,1)S(1)}, u32[]{:S(2)}, u32[]{:S(2)}) %collective-permute-start.4) | collective-permute-done | bytes 2621472 | tf_op jit(solution)/shard_map/ppermute | solution.py:103
  347.3 3.5 pad_maximum_fusion.1
  350.9 8.4 %all_to_all.18 = bf16[128,2,10240]{2,1,0:T(2,128)(2,1)} reshape(bf16[256,10240]{1,0:T(8,128)(2,1)} %pad_maximum_fusion.1) | data formatting | bytes 10485760 | tf_op jit(solution)/shard_map/all_to_all | solution.py:149
  359.3 8.3 %all-to-all-start.1 = ((bf16[128,2,10240]{2,1,0:T(2,128)(2,1)}), bf16[128,2,10240]{2,1,0:T(2,128)(2,1)}, u32[]{:S(2)}, u32[]{:S(2)}) async-start(bf16[128,2,10240]{2,1,0:T(2,128)(2,1)} %all_to_all.18), calls=%async_computation.1 | async-start | bytes 10485760 | tf_op jit(solution)/shard_map/all_to_all | solution.py:149
  367.5 64.0 %all-to-all-done.1 = bf16[128,2,10240]{2,1,0:T(2,128)(2,1)} async-done(((bf16[128,2,10240]{2,1,0:T(2,128)(2,1)}), bf16[128,2,10240]{2,1,0:T(2,128)(2,1)}, u32[]{:S(2)}, u32[]{:S(2)}) %all-to-all-start.1) | async-done | bytes 5242912 | tf_op jit(solution)/shard_map/all_to_all | solution.py:149
  431.5 7.9 %all_to_all.20 = bf16[256,10240]{1,0:T(8,128)(2,1)} reshape(bf16[128,2,10240]{2,1,0:T(2,128)(2,1)} %all-to-all-done.1) | data formatting | bytes 10485760 | tf_op jit(solution)/shard_map/all_to_all | solution.py:149
  439.4 14.0 %gather_fusion.4 = bf16[256,10240]{1,0:T(8,128)(2,1)} fusion(bf16[256,10240]{1,0:T(8,128)(2,1)} %all_to_all.20, s32[1024]{0:T(1024)S(1)} %pad_clamp_fusion), kind=kCustom, calls=%fused_computation.4 | custom fusion | bytes 10486784 | tf_op jit(solution)/shard_map/gather | solution.py:150
  453.4 5.0 %fusion.7 = (bf16[256,2560]{1,0:T(8,128)(2,1)}, bf16[256,2560]{1,0:T(8,128)(2,1)}, bf16[256,2560]{1,0:T(8,128)(2,1)}, bf16[256,2560]{1,0:T(8,128)(2,1)}) fusion(bf16[256,10240]{1,0:T(8,128)(2,1)} %gather_fusion.4), kind=kLoop, calls=%fused_computation.31 | loop fusion | bytes 10485760 | tf_op jit(solution)/shard_map/slice | solution.py:151
  (44 shorter events, 15.8 us)
Async XLA Ops:
  0.6 2.3 copy-start
  2.9 2.5 copy-start.2
  5.4 2.5 copy-start.3
  7.9 2.5 copy-start.4
  10.4 2.5 copy-start.5
  112.2 12.8 %copy-start.10 = (s32[4,1,2]{0,2,1:T(2,128)S(1)}, s32[4,1,2]{0,2,1:T(2,128)}, u32[]{:S(2)}) copy-start(s32[4,1,2]{0,2,1:T(2,128)} %param.11) | copy-start | bytes 100
  113.9 88.4 %collective-permute-start = (bf16[2,256,2560]{2,1,0:T(8,128)(2,1)}, bf16[2,256,2560]{2,1,0:T(8,128)(2,1)}, u32[]{:S(2)}, u32[]{:S(2)}) collective-permute-start(bf16[2,256,2560]{2,1,0:T(8,128)(2,1)} %pad_maximum_fusion.2), channel_id=1, source_target_pairs={{0,32},{32,64},{64,96},{1,33},{33,65},{65,97},{2,34},{34,66},{66,9... | collective-permute-start | bytes 7864328 | tf_op jit(solution)/shard_map/ppermute | solution.py:103
  117.3 91.0 %collective-permute-start.1 = (bf16[2,256,2560]{2,1,0:T(8,128)(2,1)}, bf16[2,256,2560]{2,1,0:T(8,128)(2,1)}, u32[]{:S(2)}, u32[]{:S(2)}) collective-permute-start(bf16[2,256,2560]{2,1,0:T(8,128)(2,1)} %pad_maximum_fusion.2), channel_id=1, source_target_pairs={{32,0},{64,32},{96,64},{33,1},{65,33},{97,65},{34,2},{66,34},{98,6... | collective-permute-start | bytes 7864328 | tf_op jit(solution)/shard_map/ppermute | solution.py:103
  120.3 87.9 %collective-permute-start.2 = (bf16[2,256,2560]{2,1,0:T(8,128)(2,1)}, bf16[2,256,2560]{2,1,0:T(8,128)(2,1)}, u32[]{:S(2)}, u32[]{:S(2)}) collective-permute-start(bf16[2,256,2560]{2,1,0:T(8,128)(2,1)} %pad_maximum_fusion.2), channel_id=1, source_target_pairs={{0,1},{1,2},{2,3},{3,4},{4,5},{5,6},{6,7},{7,8},{8,9},{9,10},{10,1... | collective-permute-start | bytes 7864328 | tf_op jit(solution)/shard_map/ppermute | solution.py:103
  123.7 84.5 %collective-permute-start.3 = (bf16[2,256,2560]{2,1,0:T(8,128)(2,1)}, bf16[2,256,2560]{2,1,0:T(8,128)(2,1)}, u32[]{:S(2)}, u32[]{:S(2)}) collective-permute-start(bf16[2,256,2560]{2,1,0:T(8,128)(2,1)} %pad_maximum_fusion.2), channel_id=1, source_target_pairs={{1,0},{2,1},{3,2},{4,3},{5,4},{6,5},{7,6},{8,7},{9,8},{10,9},{11,1... | collective-permute-start | bytes 7864328 | tf_op jit(solution)/shard_map/ppermute | solution.py:103
  252.2 90.9 %collective-permute-start.4 = (bf16[2,256,2560]{2,1,0:T(8,128)(2,1)}, bf16[2,256,2560]{2,1,0:T(8,128)(2,1)S(1)}, u32[]{:S(2)}, u32[]{:S(2)}) collective-permute-start(bf16[2,256,2560]{2,1,0:T(8,128)(2,1)} %get-tuple-element.15), channel_id=1, source_target_pairs={{32,0},{64,32},{96,64},{33,1},{65,33},{97,65},{34,2},{66,34},{98,6... | collective-permute-start | bytes 7864328 | tf_op jit(solution)/shard_map/ppermute | solution.py:103
  254.1 90.2 %collective-permute-start.5 = (bf16[2,256,2560]{2,1,0:T(8,128)(2,1)}, bf16[2,256,2560]{2,1,0:T(8,128)(2,1)S(1)}, u32[]{:S(2)}, u32[]{:S(2)}) collective-permute-start(bf16[2,256,2560]{2,1,0:T(8,128)(2,1)} %get-tuple-element.16), channel_id=1, source_target_pairs={{0,32},{32,64},{64,96},{1,33},{33,65},{65,97},{2,34},{34,66},{66,9... | collective-permute-start | bytes 7864328 | tf_op jit(solution)/shard_map/ppermute | solution.py:103
  259.2 85.1 %collective-permute-start.6 = (bf16[2,256,2560]{2,1,0:T(8,128)(2,1)}, bf16[2,256,2560]{2,1,0:T(8,128)(2,1)S(1)}, u32[]{:S(2)}, u32[]{:S(2)}) collective-permute-start(bf16[2,256,2560]{2,1,0:T(8,128)(2,1)} %get-tuple-element.17), channel_id=1, source_target_pairs={{1,0},{2,1},{3,2},{4,3},{5,4},{6,5},{7,6},{8,7},{9,8},{10,9},{11,1... | collective-permute-start | bytes 7864328 | tf_op jit(solution)/shard_map/ppermute | solution.py:103
  260.5 85.1 %copy-start.6 = (f32[256,2560]{1,0:T(8,128)S(1)}, f32[256,2560]{1,0:T(8,128)}, u32[]{:S(2)}) copy-start(f32[256,2560]{1,0:T(8,128)} %get-tuple-element.14) | copy-start | bytes 7864324
  260.5 85.1 %copy-start.7 = (f32[256,2560]{1,0:T(8,128)S(1)}, f32[256,2560]{1,0:T(8,128)}, u32[]{:S(2)}) copy-start(f32[256,2560]{1,0:T(8,128)} %get-tuple-element.19) | copy-start | bytes 7864324
  260.6 83.8 %collective-permute-start.7 = (bf16[2,256,2560]{2,1,0:T(8,128)(2,1)}, bf16[2,256,2560]{2,1,0:T(8,128)(2,1)S(1)}, u32[]{:S(2)}, u32[]{:S(2)}) collective-permute-start(bf16[2,256,2560]{2,1,0:T(8,128)(2,1)} %get-tuple-element.18), channel_id=1, source_target_pairs={{0,1},{1,2},{2,3},{3,4},{4,5},{5,6},{6,7},{7,8},{8,9},{9,10},{10,1... | collective-permute-start | bytes 7864328 | tf_op jit(solution)/shard_map/ppermute | solution.py:103
  345.6 1.3 copy-start.8
  345.6 1.7 copy-start.9
  359.3 72.3 %all-to-all-start.1 = ((bf16[128,2,10240]{2,1,0:T(2,128)(2,1)}), bf16[128,2,10240]{2,1,0:T(2,128)(2,1)}, u32[]{:S(2)}, u32[]{:S(2)}) async-start(bf16[128,2,10240]{2,1,0:T(2,128)(2,1)} %all_to_all.18), calls=%async_computation.1 | async-start | bytes 10485760 | tf_op jit(solution)/shard_map/all_to_all | solution.py:149
  453.4 5.0 %copy-start.1 = (bf16[256,2560]{1,0:T(8,128)(2,1)S(1)}, bf16[256,2560]{1,0:T(8,128)(2,1)}, u32[]{:S(2)}) copy-start(bf16[256,2560]{1,0:T(8,128)(2,1)} %param.6) | copy-start | bytes 3932164
